TPU v7x, 512 devices: a whole 4x4x16 slice. The times are simulated.
512 devices in a mesh: ctx: 64 (over z, x_lo, core), tp: 8 (over y, x_hi).
Axes of the slice: x: 4 (x_hi: 2, x_lo: 2; x = x_hi * 2 + x_lo), y: 4, z: 16, core: 2. Of those that a mesh axis runs over, the one named last changes fastest.
Arguments:
- queries: bfloat16 [8192, 4096], P('ctx', 'tp'), may hold values from -5 to 5
- keys: bfloat16 [8192, 1024], P('ctx', 'tp'), may hold values from -5 to 5
- values: bfloat16 [8192, 1024], P('ctx', 'tp'), may hold values from -6 to 6
- docs: int32 [8192], P('ctx'), may hold values from 0 to 11, never falling along the last dimension, each value on 1 to 4224 neighbouring positions
- out_weight: bfloat16 [4096, 4096], P('tp'), may hold values from -0.09375 to 0.09375
Outputs:
- mixed: bfloat16 [8192, 4096], P('ctx', 'tp')
All inputs are finite; a program needn't handle non-finite values.
Results may differ from a plain program's by a relative error of at most 0.014.
Values may be sent and summed in bfloat16 or wider, within the bound.
No kernel may reach another device: no remote copies, remote signals or barrier semaphores. Data moves between devices by JAX's collectives and lax.ppermute only.
A program may use at most 64 MiB of HBM per device.

v0:
```python
import math
import jax
import jax.numpy as jnp
from jax import lax
from jax.sharding import PartitionSpec as P

HEAD_DIM = 128
neg_large = -1e30


def attend(state, query_half, query_pos, query_doc, key_part, value_part, key_pos, key_doc):
    peak, total, accum = state
    scores = jnp.einsum("igkd,jgd->gkij", query_half, key_part, preferred_element_type=jnp.float32)
    scores = scores * (1.0 / math.sqrt(key_part.shape[-1]))
    allowed = (key_pos[None, :] <= query_pos[:, None]) & (key_doc[None, :] == query_doc[:, None])
    block_peak = jnp.max(jnp.where(allowed, scores, neg_large), axis=-1)
    new_peak = jnp.maximum(peak, block_peak)
    rescale = jnp.exp(peak - new_peak)
    weights = jnp.where(allowed, jnp.exp(scores - new_peak[..., None]), 0.0)
    total = total * rescale + jnp.sum(weights, axis=-1)
    update = jnp.einsum(
        "gkij,jgd->gkid",
        weights.astype(jnp.bfloat16),
        value_part,
        preferred_element_type=jnp.float32,
    )
    accum = accum * rescale[..., None] + update
    return (new_peak, total, accum)


def visit(state, query_half, query_pos, query_doc, key_part, value_part, key_pos, key_doc):
    needed = jnp.min(key_pos) <= jnp.max(query_pos)

    def compute(current):
        return attend(
            current, query_half, query_pos, query_doc, key_part, value_part, key_pos, key_doc
        )

    def unchanged(current):
        return current

    return lax.cond(needed, compute, unchanged, state)


def finish(state):
    peak, total, accum = state
    summed = accum / total[..., None]
    kv_count, group_size, row_count, head_dim = summed.shape
    summed = jnp.transpose(summed, (2, 0, 1, 3)).reshape(
        row_count, kv_count * group_size * head_dim
    )
    return summed.astype(jnp.bfloat16)


def shards(queries, keys, values, docs, out_weight):
    row_count = queries.shape[0]
    half_rows = row_count // 2
    head_dim = HEAD_DIM
    kv_local = keys.shape[1] // head_dim
    group_size = queries.shape[1] // keys.shape[1]
    my_index = lax.axis_index("ctx")
    all_docs = lax.all_gather(docs, "ctx", axis=0, tiled=True)
    offsets = jnp.arange(half_rows, dtype=jnp.int32)
    shard_offsets = jnp.arange(row_count, dtype=jnp.int32)
    lower_queries = queries[:half_rows]
    upper_queries = queries[half_rows:]
    low_positions = my_index * row_count + offsets
    high_positions = my_index * row_count + half_rows + offsets
    low_docs = jnp.take(all_docs, low_positions)
    high_docs = jnp.take(all_docs, high_positions)
    query_low = lower_queries.reshape(half_rows, kv_local, group_size, head_dim)
    query_high = upper_queries.reshape(half_rows, kv_local, group_size, head_dim)
    empty = (
        jnp.full((kv_local, group_size, half_rows), neg_large, jnp.float32),
        jnp.zeros((kv_local, group_size, half_rows), jnp.float32),
        jnp.zeros((kv_local, group_size, half_rows, head_dim), jnp.float32),
    )
    carry = (empty, empty)
    key_piece = lax.all_gather(keys, "ctx", axis=0, tiled=True)
    value_piece = lax.all_gather(values, "ctx", axis=0, tiled=True)
    shard_count = key_piece.shape[0] // row_count
    shaped_keys = key_piece.reshape(shard_count, row_count, kv_local, head_dim)
    shaped_values = value_piece.reshape(shard_count, row_count, kv_local, head_dim)
    shard_numbers = jnp.arange(shard_count, dtype=jnp.int32)

    def one_shard(states, inputs):
        key_part, value_part, shard_number = inputs
        key_pos = shard_number * row_count + shard_offsets
        key_doc = jnp.take(all_docs, key_pos)
        state_low, state_high = states
        state_low = visit(
            state_low, query_low, low_positions, low_docs, key_part, value_part, key_pos, key_doc
        )
        state_high = visit(
            state_high,
            query_high,
            high_positions,
            high_docs,
            key_part,
            value_part,
            key_pos,
            key_doc,
        )
        return ((state_low, state_high), None)

    carry, unused = lax.scan(one_shard, carry, (shaped_keys, shaped_values, shard_numbers))
    attention = jnp.concatenate([finish(carry[0]), finish(carry[1])], axis=0)
    partial_terms = jnp.dot(attention, out_weight, preferred_element_type=jnp.float32)
    mixed = lax.psum_scatter(
        partial_terms.astype(jnp.bfloat16), "tp", scatter_dimension=1, tiled=True
    )
    return mixed


def solution(mesh):
    placed = (P("ctx", "tp"), P("ctx", "tp"), P("ctx", "tp"), P("ctx"), P("tp", None))
    return jax.shard_map(
        shards, mesh=mesh, in_specs=placed, out_specs=P("ctx", "tp"), check_vma=False
    )
```

profile of v0, /device:TPU:32, one launch (start us, length us, event | category | flops | bytes accessed | tf_op | source)
XLA Modules:
  0.0 863.5 jit_solution(10624895469857638994)
XLA Ops:
  8.1 66.9 %all-gather = s32[64,1,128]{2,1,0:T(1,128)S(1)} all-gather(s32[1,1,128]{2,1,0:T(1,128)} %bitcast.123), channel_id=1, replica_groups=mesh['ctx'=64,'tp'=8] {'ctx'}, dimensions={0}, use_global_device_ids=true | all-gather | bytes 33280 | tf_op jit(solution)/shard_map/all_gather | solution.py:62
  78.2 57.6 %all-gather.4.cloned.1.call-done = bf16[8192,128]{1,0:T(8,128)(2,1)} async-done(((bf16[128,128]{1,0:T(8,128)(2,1)}), bf16[8192,128]{1,0:T(8,128)(2,1)}) %all-gather.4.cloned.1.call-update) | async-done | bytes 2097168 | tf_op jit(solution)/shard_map/all_gather | solution.py:79
  135.9 120.6 %all-gather.6.cloned.1.call-done = bf16[8192,128]{1,0:T(8,128)(2,1)} async-done(((bf16[128,128]{1,0:T(8,128)(2,1)}), bf16[8192,128]{1,0:T(8,128)(2,1)}) %all-gather.6.cloned.1.call-update) | async-done | bytes 2097168 | tf_op jit(solution)/shard_map/all_gather | solution.py:80
  256.6 417.2 %while.22 = (s32[]{:T(128)}, f32[1,4,64]{2,1,0:T(4,128)S(1)}, f32[1,4,64]{2,1,0:T(4,128)S(1)}, f32[1,4,64,128]{3,2,1,0:T(8,128)S(1)}, f32[1,4,64]{2,1,0:T(4,128)...) while((s32[]{:T(128)}, f32[1,4,64]{2,1,0:T(4,128)S(1)}, ...), condition=%wide.region_12.14_spmd.clone, body=%wide.region_2.13_spmd.clone.sunk | while | flops 34328964 | bytes 1815597 | solution.py:106
  257.8 1.1 gather_fusion
  265.9 1.1 gather_fusion
  274.0 1.1 gather_fusion
  282.1 1.1 gather_fusion
  290.2 1.1 gather_fusion
  298.2 1.1 gather_fusion
  304.6 1.1 gather_fusion
  311.0 1.1 gather_fusion
  317.4 1.1 gather_fusion
  323.8 1.1 gather_fusion
  330.2 1.1 gather_fusion
  336.6 1.1 gather_fusion
  342.9 1.1 gather_fusion
  349.3 1.1 gather_fusion
  355.7 1.1 gather_fusion
  362.1 1.1 gather_fusion
  368.5 1.1 gather_fusion
  374.9 1.1 gather_fusion
  381.3 1.1 gather_fusion
  387.6 1.1 gather_fusion
  394.0 1.1 gather_fusion
  400.4 1.1 gather_fusion
  406.8 1.1 gather_fusion
  413.2 1.1 gather_fusion
  489.8 1.1 gather_fusion
  611.1 1.1 gather_fusion
  674.1 3.9 convolution_convert_fusion
  678.1 178.9 %reduce-scatter.2.cloned.1.call-done = bf16[128,512]{1,0:T(8,128)(2,1)} async-done(((bf16[128,4096]{1,0:T(8,128)(2,1)}), bf16[128,512]{1,0:T(8,128)(2,1)}) %reduce-scatter.2.cloned.1.call-update) | async-done | bytes 131088 | tf_op jit(solution)/shard_map/reduce_scatter | solution.py:109
  (790 shorter events, 199.1 us)
Async XLA Ops:
  6.5 129.3 %all-gather.4.cloned.1.call-start = ((), (), s32[]{:S(2)}) async-start(), calls=%async_computation.1 | async-start | bytes 2129920 | tf_op jit(solution)/shard_map/all_gather | solution.py:79
  7.3 249.2 %all-gather.6.cloned.1.call-start = ((), (), s32[]{:S(2)}) async-start(), calls=%async_computation.2 | async-start | bytes 2129920 | tf_op jit(solution)/shard_map/all_gather | solution.py:80
  8.0 849.0 %reduce-scatter.2.cloned.1.call-start = ((), (), s32[]{:S(2)}) async-start(), calls=%async_computation.3 | async-start | bytes 1179648 | tf_op jit(solution)/shard_map/reduce_scatter | solution.py:109
Sparse Core Ops, SparseCore 0:
  9.5 126.3 all-gather.3
  138.0 118.4 all-gather.5
  678.2 178.6 reduce-scatter.1
where the time goes:
time: 871 us; the launch traced here: 863 us
  waiting for transfers between devices  359 us (41%)
  loops' own time  203 us (23%)
  local copies, waits for them, and re-layouts  165 us (19%)
  blocking collectives  66.9 us (8%)
  other arithmetic  47.5 us (5%)
  between operations  13.2 us (2%)
  matrix products  9.02 us (1%)
    another operation x1, loops' own time, shards(): lax.scan(one_shard, carry, (shaped_keys, shaped_values, shard_numbers))  201 us
    reduce_scatter x1, waiting for transfers between devices, shards(): lax.psum_scatter(partial_terms.astype(jnp.bfloat16), 'tp', scatter_dimens...  179 us
    all_gather x1, waiting for transfers between devices, shards(): value_piece = lax.all_gather(values, 'ctx', axis=0, tiled=True)  121 us
    gather x64, local copies, waits for them, and re-layouts, one_shard(): key_doc = jnp.take(all_docs, key_pos)  73.5 us
    all_gather x1, blocking collectives, shards(): all_docs = lax.all_gather(docs, 'ctx', axis=0, tiled=True)  66.9 us
    all_gather x1, waiting for transfers between devices, shards(): key_piece = lax.all_gather(keys, 'ctx', axis=0, tiled=True)  57.6 us
    squeeze x64, local copies, waits for them, and re-layouts, shards(): lax.scan(one_shard, carry, (shaped_keys, shaped_values, shard_numbers))  50.4 us
    reduce_min x64, other arithmetic, visit(): needed = jnp.min(key_pos) <= jnp.max(query_pos)  42.4 us
  transfers between devices with their start and end apart: 3, of which 3 were waited for; matrix products, arithmetic and copies ran while one was open for 0% of the time, Pallas kernels for 0%

commit v1 on v0

--- a/solution.py
+++ b/solution.py
@@ -53,6 +53,12 @@
 
 
 def shards(queries, keys, values, docs, out_weight):
+
+    def _render_indices(a_name, frame, local_x):
+        tile_out = jnp.concatenate([local_x, frame], axis=1)
+        inter = lax.all_gather(tile_out, a_name, axis=0, tiled=True)
+        return jnp.split(inter, [local_x.shape[1]], axis=1)
+
     row_count = queries.shape[0]
     half_rows = row_count // 2
     head_dim = HEAD_DIM
@@ -76,8 +82,7 @@
         jnp.zeros((kv_local, group_size, half_rows, head_dim), jnp.float32),
     )
     carry = (empty, empty)
-    key_piece = lax.all_gather(keys, "ctx", axis=0, tiled=True)
-    value_piece = lax.all_gather(values, "ctx", axis=0, tiled=True)
+    key_piece, value_piece = _render_indices("ctx", values, keys)
     shard_count = key_piece.shape[0] // row_count
     shaped_keys = key_piece.reshape(shard_count, row_count, kv_local, head_dim)
     shaped_values = value_piece.reshape(shard_count, row_count, kv_local, head_dim)

time: 871 us -> 774 us (0.89)
  waiting for transfers between devices: 359 us -> 238 us
  loops' own time: 203 us -> 218 us
    all_gather x2 -> x1, waiting for transfers between devices: 178 us -> 59.4 us  [_render_indices(): inter = lax.all_gather(tile_out, a_name, axis=0, tiled=True)]
    another operation x1, loops' own time: 201 us -> 216 us  [shards(): lax.scan(one_shard, carry, (shaped_keys, shaped_values, shard_numbers))]
  transfers between devices with their start and end apart: 3 -> 2, of which waited for: 3 -> 2; matrix products, arithmetic and copies ran while one was open for 0% -> 1% of each run, Pallas kernels for 0% -> 0%
where the time goes in v1:
time: 774 us; the launch traced here: 766 us
  waiting for transfers between devices  238 us (31%)
  loops' own time  218 us (28%)
  local copies, waits for them, and re-layouts  167 us (22%)
  blocking collectives  66.9 us (9%)
  other arithmetic  52.7 us (7%)
  between operations  13.5 us (2%)
  matrix products  9.04 us (1%)
    another operation x1, loops' own time, shards(): lax.scan(one_shard, carry, (shaped_keys, shaped_values, shard_numbers))  216 us
    reduce_scatter x1, waiting for transfers between devices, shards(): lax.psum_scatter(partial_terms.astype(jnp.bfloat16), 'tp', scatter_dimens...  179 us
    gather x64, local copies, waits for them, and re-layouts, one_shard(): key_doc = jnp.take(all_docs, key_pos)  73.5 us
    all_gather x1, blocking collectives, shards(): all_docs = lax.all_gather(docs, 'ctx', axis=0, tiled=True)  66.9 us
    all_gather x1, waiting for transfers between devices, _render_indices(): inter = lax.all_gather(tile_out, a_name, axis=0, tiled=True)  59.4 us
    squeeze x64, local copies, waits for them, and re-layouts, shards(): lax.scan(one_shard, carry, (shaped_keys, shaped_values, shard_numbers))  49.3 us
    reduce_min x64, other arithmetic, visit(): needed = jnp.min(key_pos) <= jnp.max(query_pos)  45.5 us
    dynamic_slice x64, local copies, waits for them, and re-layouts, shards(): lax.scan(one_shard, carry, (shaped_keys, shaped_values, shard_numbers))  37.6 us
  transfers between devices with their start and end apart: 2, of which 2 were waited for; matrix products, arithmetic and copies ran while one was open for 1% of the time, Pallas kernels for 0%

profile of v1, /device:TPU:32, one launch (start us, length us, event | category | flops | bytes accessed | tf_op | source)
XLA Modules:
  0.0 766.0 jit_solution(10819931098444831321)
XLA Ops:
  6.5 1.4 pad_maximum_fusion
  8.0 66.9 %all-gather = s32[64,1,128]{2,1,0:T(1,128)S(1)} all-gather(s32[1,1,128]{2,1,0:T(1,128)} %bitcast.123), channel_id=1, replica_groups=mesh['ctx'=64,'tp'=8] {'ctx'}, dimensions={0}, use_global_device_ids=true | all-gather | bytes 33280 | tf_op jit(solution)/shard_map/all_gather | solution.py:68
  78.8 59.4 %all-gather.3.cloned.1.call-done = bf16[8192,256]{1,0:T(8,128)(2,1)} async-done(((bf16[128,256]{1,0:T(8,128)(2,1)}), bf16[8192,256]{1,0:T(8,128)(2,1)}) %all-gather.3.cloned.1.call-update) | async-done | bytes 4194320 | tf_op jit(solution)/shard_map/all_gather | solution.py:59
  138.2 3.8 fusion.44
  142.1 433.7 %while.22 = (s32[]{:T(128)}, f32[1,4,64]{2,1,0:T(4,128)S(1)}, f32[1,4,64]{2,1,0:T(4,128)S(1)}, f32[1,4,64,128]{3,2,1,0:T(8,128)S(1)}, f32[1,4,64]{2,1,0:T(4,128)...) while((s32[]{:T(128)}, f32[1,4,64]{2,1,0:T(4,128)S(1)}, ...), condition=%wide.region_12.14_spmd.clone, body=%wide.region_2.13_spmd.clone.sunk | while | flops 34328964 | bytes 1815597 | solution.py:111
  143.4 1.1 gather_fusion
  151.7 1.1 gather_fusion
  160.0 1.1 gather_fusion
  168.4 1.1 gather_fusion
  176.7 1.1 gather_fusion
  185.1 1.1 gather_fusion
  191.7 1.1 gather_fusion
  198.4 1.1 gather_fusion
  205.0 1.1 gather_fusion
  211.7 1.1 gather_fusion
  218.3 1.1 gather_fusion
  224.9 1.1 gather_fusion
  231.6 1.1 gather_fusion
  238.2 1.1 gather_fusion
  244.9 1.1 gather_fusion
  251.5 1.1 gather_fusion
  258.2 1.1 gather_fusion
  264.8 1.1 gather_fusion
  271.5 1.1 gather_fusion
  278.1 1.1 gather_fusion
  284.7 1.1 gather_fusion
  291.4 1.1 gather_fusion
  298.0 1.1 gather_fusion
  397.7 1.1 gather_fusion
  523.9 1.1 gather_fusion
  576.2 4.0 convolution_convert_fusion
  580.2 179.0 %reduce-scatter.2.cloned.1.call-done = bf16[128,512]{1,0:T(8,128)(2,1)} async-done(((bf16[128,4096]{1,0:T(8,128)(2,1)}), bf16[128,512]{1,0:T(8,128)(2,1)}) %reduce-scatter.2.cloned.1.call-update) | async-done | bytes 131088 | tf_op jit(solution)/shard_map/reduce_scatter | solution.py:114
  (789 shorter events, 201.2 us)
Async XLA Ops:
  6.5 131.6 %all-gather.3.cloned.1.call-start = ((), (), s32[]{:S(2)}) async-start(), calls=%async_computation.1 | async-start | bytes 4259840 | tf_op jit(solution)/shard_map/all_gather | solution.py:59
  8.0 751.2 %reduce-scatter.2.cloned.1.call-start = ((), (), s32[]{:S(2)}) async-start(), calls=%async_computation.2 | async-start | bytes 1179648 | tf_op jit(solution)/shard_map/reduce_scatter | solution.py:114
Sparse Core Ops, SparseCore 0:
  9.5 128.6 all-gather.2
  580.3 178.8 reduce-scatter.1
